TPU v7x, 32 devices: a whole 2x2x4 slice. The times are simulated.
32 devices in a mesh: seq: 8 (over z, x), tp: 4 (over y, core).
Axes of the slice: x: 2, y: 2, z: 4, core: 2. Of those that a mesh axis runs over, the one named last changes fastest.
Arguments:
- queries: bfloat16 [1024, 4096], P('seq', 'tp'), may hold values from -600 to 600
- suffix_keys: bfloat16 [1024, 1024], P('seq', 'tp'), may hold values from -6 to 6
- suffix_values: bfloat16 [1024, 1024], P('seq', 'tp'), may hold values from -6 to 6
- prefix_keys: bfloat16 [512, 1024], P('seq', 'tp'), may hold values from -6 to 6
- prefix_values: bfloat16 [512, 1024], P('seq', 'tp'), may hold values from -6 to 6
- suffix_lengths: int32 [24], replicated, may hold values from 1 to 128, 1024 in all
- request_group: int32 [24], replicated, may hold values from 0 to 3
- block_group: int32 [8], replicated, may hold values from 0 to 3, as said below
Outputs:
- attended: bfloat16 [1024, 4096], P('seq', 'tp')
- cache_keys: bfloat16 [1024, 1024], P(('seq', 'tp'))
- cache_values: bfloat16 [1024, 1024], P(('seq', 'tp'))
Inputs may be any that keep to these rules, and one draw needn't show every extreme that they name: `suffix_lengths`: the suffixes fill the 1024 packed tokens end to end in order; the longest has exactly 128 tokens. `block_group`: each prefix is held by exactly 2 blocks, in any order.
All inputs are finite; a program needn't handle non-finite values.
Results may differ from a plain program's by a relative error of at most 0.009.
The roundings to bfloat16 on the way count: a program that leaves them out, or rounds other values in their place, can miss the bound.
Values may be sent and summed in bfloat16 or wider, within the bound.
No kernel may reach another device: no remote copies, remote signals or barrier semaphores. Data moves between devices by JAX's collectives and lax.ppermute only.
A program may use at most 64 MiB of HBM per device.

v0:
```python
import math
import jax
import jax.numpy as jnp
from jax import lax
from jax.sharding import PartitionSpec as P

HD = 128
GROUPS = 4
BIG_NEGATIVE = -1e30


def from_behind(array, axis, by):
    length = lax.axis_size(axis)
    pairs = [(i, i + by) for i in range(length) if 0 <= i + by < length]
    return lax.ppermute(array, axis, pairs)


def rotate(values, position):
    half = values.shape[-1] // 2
    freq = jnp.exp(
        jnp.arange(half, dtype=jnp.float32) * (-2.0 * math.log(500000.0) / values.shape[-1])
    )
    angle = position.astype(jnp.float32)[:, None] * freq[None, :]
    cosine = jnp.cos(angle)[:, None, :]
    sine = jnp.sin(angle)[:, None, :]
    floats = values.astype(jnp.float32)
    lower = floats[..., :half]
    upper = floats[..., half:]
    return jnp.concatenate(
        [lower * cosine - upper * sine, upper * cosine + lower * sine], axis=-1
    ).astype(jnp.bfloat16)


def token_info(index, suffix_lengths, request_group):
    ends = jnp.cumsum(suffix_lengths)
    request = jnp.sum((index[:, None] >= ends[None, :]).astype(jnp.int32), axis=1)
    onehot = request[:, None] == jnp.arange(suffix_lengths.shape[0], dtype=jnp.int32)[None, :]
    first = jnp.sum(jnp.where(onehot, (ends - suffix_lengths)[None, :], 0), axis=1)
    group = jnp.sum(jnp.where(onehot, request_group[None, :], 0), axis=1)
    return (request, index - first, group)


def body(
    queries,
    suffix_keys,
    suffix_values,
    prefix_keys,
    prefix_values,
    suffix_lengths,
    request_group,
    block_group,
):
    rows = queries.shape[0]
    kv_cols = suffix_keys.shape[1]
    kv_heads = kv_cols // HD
    q_heads = queries.shape[1] // HD
    repeat = q_heads // kv_heads
    devices = lax.axis_size("seq")
    me = lax.axis_index("seq")
    block_rows = prefix_keys.shape[0]
    prefix_len = block_rows * devices // GROUPS
    span = max(1, min(2048 // rows, devices // 8))
    scale = HD ** (-0.5)
    index = me * rows + jnp.arange(rows, dtype=jnp.int32)
    request, offset, group = token_info(index, suffix_lengths, request_group)
    position = offset + prefix_len
    q_rot = rotate(queries.reshape(rows, q_heads, HD), position).reshape(rows, kv_heads, repeat, HD)
    k_rot = rotate(suffix_keys.reshape(rows, kv_heads, HD), position).reshape(rows, kv_cols)

    def update(carry, keys, values, visible):
        high, total, accum = carry
        keys_split = keys.reshape(keys.shape[0], kv_heads, HD)
        values_split = values.reshape(values.shape[0], kv_heads, HD)
        scores = (
            jnp.einsum("bgrd,kgd->bgrk", q_rot, keys_split, preferred_element_type=jnp.float32)
            * scale
        )
        mask = visible[:, None, None, :]
        scores = jnp.where(mask, scores, BIG_NEGATIVE)
        new_high = jnp.maximum(high, jnp.max(scores, axis=-1))
        weights = jnp.where(mask, jnp.exp(scores - new_high[..., None]), 0.0)
        factor = jnp.exp(high - new_high)
        total = total * factor + jnp.sum(weights, axis=-1)
        accum = accum * factor[..., None] + jnp.einsum(
            "bgrk,kgd->bgrd",
            weights.astype(jnp.bfloat16),
            values_split,
            preferred_element_type=jnp.float32,
        )
        return (new_high, total, accum)

    def guarded(carry, keys, values, visible):
        return update(carry, keys, values, visible)

    def suffix_visible(back):
        key_index = (me - back) * rows + jnp.arange(rows, dtype=jnp.int32)
        key_request, _, _ = token_info(key_index, suffix_lengths, request_group)
        return (
            (key_index[None, :] >= 0)
            & (key_request[None, :] == request[:, None])
            & (key_index[None, :] <= index[:, None])
        )

    start_state = (
        jnp.full((rows, kv_heads, repeat), BIG_NEGATIVE, jnp.float32),
        jnp.zeros((rows, kv_heads, repeat), jnp.float32),
        jnp.zeros((rows, kv_heads, repeat, HD), jnp.float32),
    )
    carry = start_state
    keys = lax.all_gather(prefix_keys, "seq", axis=0, tiled=True)
    values = lax.all_gather(prefix_values, "seq", axis=0, tiled=True)
    count = keys.shape[0]
    width = 512

    def one_step(state, step):
        first = step * width
        keys_part = lax.dynamic_slice_in_dim(keys, first, width, 0)
        values_part = lax.dynamic_slice_in_dim(values, first, width, 0)
        row_index = first + jnp.arange(width, dtype=jnp.int32)
        holder = row_index // block_rows
        matches = holder[:, None] == jnp.arange(block_group.shape[0], dtype=jnp.int32)[None, :]
        row_group = jnp.sum(jnp.where(matches, block_group[None, :], 0), axis=1)
        visible = row_group[None, :] == group[:, None]
        return (guarded(state, keys_part, values_part, visible), None)

    carry, _ = lax.scan(one_step, carry, jnp.arange(count // width, dtype=jnp.int32))
    carry = guarded(carry, k_rot, suffix_values, suffix_visible(0))
    for back in range(1, span + 1):
        earlier_keys, earlier_values = from_behind((k_rot, suffix_values), "seq", back)
        carry = guarded(carry, earlier_keys, earlier_values, suffix_visible(back))
    high, total, accum = carry
    attended = (accum / total[..., None]).reshape(rows, q_heads * HD).astype(jnp.bfloat16)
    cache_keys, cache_values = (
        lax.all_to_all(k_rot, "tp", split_axis=0, concat_axis=1, tiled=True),
        lax.all_to_all(suffix_values, "tp", split_axis=0, concat_axis=1, tiled=True),
    )
    return (attended, cache_keys, cache_values)


def solution(mesh):
    return jax.shard_map(
        body,
        mesh=mesh,
        in_specs=(
            P("seq", "tp"),
            P("seq", "tp"),
            P("seq", "tp"),
            P("seq", "tp"),
            P("seq", "tp"),
            P(),
            P(),
            P(),
        ),
        out_specs=(P("seq", "tp"), P(("seq", "tp"), None), P(("seq", "tp"), None)),
        check_vma=False,
    )
```

profile of v0, /device:TPU:0, one launch (start us, length us, event | category | flops | bytes accessed | tf_op | source)
XLA Modules:
  0.0 101.6 jit_solution(3033059807300362979)
XLA Ops:
  0.7 0.8 copy.95
  1.6 0.7 sub.87
  2.4 0.7 select_reduce_fusion.2
  3.1 0.9 copy.101
  4.3 0.3 multiply_cosine_fusion
  4.7 0.7 copy.106
  5.5 5.5 %collective-permute-start = (bf16[128,256]{0,1:T(8,128)(2,1)}, bf16[128,256]{0,1:T(8,128)(2,1)}, u32[]{:S(2)}, u32[]{:S(2)}) collective-permute-start(bf16[128,256]{0,1:T(8,128)(2,1)} %bitcast.19), channel_id=1, source_target_pairs={{0,4},{4,8},{8,12},{12,16},{16,20},{20,24},{24,28},{1,5},{5,9},{9,... | collective-permute-start | bytes 196616 | tf_op jit(solution)/shard_map/ppermute | solution.py:15
  10.9 3.5 %collective-permute-start.1 = (bf16[128,256]{1,0:T(8,128)(2,1)}, bf16[128,256]{1,0:T(8,128)(2,1)}, u32[]{:S(2)}, u32[]{:S(2)}) collective-permute-start(bf16[128,256]{1,0:T(8,128)(2,1)} %param.10), channel_id=1, source_target_pairs={{0,4},{4,8},{8,12},{12,16},{16,20},{20,24},{24,28},{1,5},{5,9},{9,... | collective-permute-start | bytes 196616 | tf_op jit(solution)/shard_map/ppermute | solution.py:15
  14.5 0.7 convert_element_type.70
  15.2 3.3 %all-to-all-start = ((bf16[4,32,256]{2,1,0:T(8,128)(2,1)}), bf16[4,32,256]{2,1,0:T(8,128)(2,1)S(1)}, u32[]{:S(2)}, u32[]{:S(2)}) async-start(bf16[4,32,256]{2,1,0:T(8,128)(2,1)} %convert_element_type.70), calls=%async_computation | async-start | bytes 131072 | tf_op jit(solution)/shard_map/all_to_all | solution.py:134
  18.7 0.2 fusion.46
  18.9 31.0 %all_gather.6 = bf16[512,256]{1,0:T(8,128)(2,1)S(1)} all-gather(bf16[64,256]{1,0:T(8,128)(2,1)S(1)} %copy-done.7), channel_id=1, replica_groups=mesh['seq'=8,'tp'=4] {'seq'}, dimensions={0}, use_global_device_ids=true | all-gather | bytes 294912 | tf_op jit(solution)/shard_map/all_gather | solution.py:110
  49.8 0.1 copy.98
  50.0 0.2 subtract_convert_fusion
  50.4 0.8 compare_and_fusion
  51.2 1.2 %bitcast_reduce_fusion = (f32[128,2,4]{0,2,1:T(4,128)}, f32[2,128,4,512]{3,1,2,0:T(8,128)S(1)}) fusion(pred[128,512]{1,0:T(8,128)(4,1)S(1)} %broadcast_compare_fusion, bf16[512,2,128,1]{0,2,3,1:T(8,128)(2,1)S(1)} %bitcast.101, bf16[128,2,4,64]{3,0,2,1:T(8,128)(2,1)S(1)} %bitcast.98, bf16[128,2,4,64]{3,0,2,1:T(8,128)(2,1)S(1)} %bitcast.95), kind=kOutput, calls=%fused_computation.1 | convolution fusion | flops 136313856 | bytes 2691072 | tf_op jit(solution)/shard_map/while/body/eval_jaxpr/bgrd,kgd->bgrk/dot_general | solution.py:75
  52.4 0.9 fusion.49
  53.3 0.6 copy-done.4
  53.9 3.9 %all-to-all-start.1 = ((bf16[4,32,256]{2,1,0:T(8,128)(2,1)}), bf16[4,32,256]{2,1,0:T(8,128)(2,1)}, u32[]{:S(2)}, u32[]{:S(2)}) async-start(bf16[4,32,256]{2,1,0:T(8,128)(2,1)} %bitcast.29), calls=%async_computation.1 | async-start | bytes 131072 | tf_op jit(solution)/shard_map/all_to_all | solution.py:135
  57.8 31.0 %all_gather.7 = bf16[512,256]{1,0:T(8,128)(2,1)S(1)} all-gather(bf16[64,256]{1,0:T(8,128)(2,1)} %param.12), channel_id=1, replica_groups=mesh['seq'=8,'tp'=4] {'seq'}, dimensions={0}, use_global_device_ids=true | all-gather | bytes 294912 | tf_op jit(solution)/shard_map/all_gather | solution.py:111
  88.9 0.9 copy.124
  89.8 0.8 copy.100
  90.7 1.5 %copy.131 = bf16[4,4,8,256]{3,2,0,1:T(8,128)(2,1)} copy(bf16[4,4,8,256]{3,2,1,0:T(8,128)(2,1)} %bitcast.106) | data formatting | bytes 131072 | tf_op jit(solution)/shard_map/all_to_all | solution.py:134
  92.2 1.5 %copy.132 = bf16[4,4,8,256]{3,2,0,1:T(8,128)(2,1)} copy(bf16[4,4,8,256]{3,2,1,0:T(8,128)(2,1)} %bitcast.46) | data formatting | bytes 131072 | tf_op jit(solution)/shard_map/all_to_all | solution.py:135
  93.6 1.2 %fusion.48 = (f32[128,2,4]{0,2,1:T(4,128)S(1)}, f32[128,2,4,128]{0,3,2,1:T(8,128)S(1)}) fusion(bf16[128,2,128,1]{0,2,3,1:T(8,128)(2,1)} %bitcast.39, bf16[128,2,4,64]{3,0,2,1:T(8,128)(2,1)S(1)} %bitcast.100, bf16[128,2,4,64]{3,0,2,1:T(8,128)(2,1)S(1)} %bitcast.97, pred[128,128]{0,1:T(8,128)(4,1)} %get-tuple-element.67), kind=kOutput, calls=%fused_computation.88 | convolution fusion | flops 34470912 | bytes 872448 | tf_op jit(solution)/shard_map/bgrd,kgd->bgrk/dot_general | solution.py:75
  94.9 0.7 fusion.44
  95.7 0.2 convolution_bitcast_fusion.1
  96.0 0.7 fusion.2
  96.9 1.6 %fusion.7 = f32[128,2,4,128]{0,3,2,1:T(8,128)} fusion(f32[128,2,4,128]{0,3,2,1:T(8,128)S(1)} %convolution_bitcast_fusion.1, bf16[512,2,128,1]{0,2,3,1:T(8,128)(2,1)S(1)} %bitcast.104, f32[2,128,4,512]{3,1,2,0:T(8,128)S(1)} %get-tuple-element.76, f32[128,2,4]{0,2,1:T(4,128)S(1)} %get-tuple-element.66, pred[128,512]{1,0:T(8,128)(4,1)S(1)} %broadcast_compare_fusion, ...), kind=kOutput, calls=%fused_computation.13 | convolution fusion | flops 137363456 | bytes 3489792 | tf_op jit(solution)/shard_map/while/body/eval_jaxpr/bgrk,kgd->bgrd/dot_general | solution.py:84
  98.5 0.9 copy.108
  99.4 1.3 %fusion.14 = bf16[128,2,4,128]{0,3,2,1:T(8,128)(2,1)S(1)} fusion(f32[128,2,4,128]{0,3,2,1:T(8,128)} %fusion.7, bf16[128,2,128,1]{0,2,3,1:T(8,128)(2,1)S(1)} %bitcast.109, f32[128,2,4,128]{0,3,2,1:T(8,128)S(1)} %copy-done.1, f32[128,2,4]{0,2,1:T(4,128)S(1)} %get-tuple-element.52, f32[128,2,4]{0,2,1:T(4,128)S(1)} %get-tuple-element.55, ...), kind=kOutput, calls=%fused_computation.22 | convolution fusion | flops 34340864 | bytes 1400832 | tf_op jit(solution)/shard_map/bgrk,kgd->bgrd/dot_general | solution.py:84
  100.7 0.9 copy.113
  (42 shorter events, 1.3 us)
Async XLA Ops:
  0.6 17.9 %copy-start.2 = (bf16[128,1024]{1,0:T(8,128)(2,1)S(1)}, bf16[128,1024]{1,0:T(8,128)(2,1)}, u32[]{:S(2)}) copy-start(bf16[128,1024]{1,0:T(8,128)(2,1)} %param.8) | copy-start | bytes 786436
  5.5 88.2 %collective-permute-start = (bf16[128,256]{0,1:T(8,128)(2,1)}, bf16[128,256]{0,1:T(8,128)(2,1)}, u32[]{:S(2)}, u32[]{:S(2)}) collective-permute-start(bf16[128,256]{0,1:T(8,128)(2,1)} %bitcast.19), channel_id=1, source_target_pairs={{0,4},{4,8},{8,12},{12,16},{16,20},{20,24},{24,28},{1,5},{5,9},{9,... | collective-permute-start | bytes 196616 | tf_op jit(solution)/shard_map/ppermute | solution.py:15
  10.9 87.5 %collective-permute-start.1 = (bf16[128,256]{1,0:T(8,128)(2,1)}, bf16[128,256]{1,0:T(8,128)(2,1)}, u32[]{:S(2)}, u32[]{:S(2)}) collective-permute-start(bf16[128,256]{1,0:T(8,128)(2,1)} %param.10), channel_id=1, source_target_pairs={{0,4},{4,8},{8,12},{12,16},{16,20},{20,24},{24,28},{1,5},{5,9},{9,... | collective-permute-start | bytes 196616 | tf_op jit(solution)/shard_map/ppermute | solution.py:15
  14.5 4.4 %copy-start.7 = (bf16[64,256]{1,0:T(8,128)(2,1)S(1)}, bf16[64,256]{1,0:T(8,128)(2,1)}, u32[]{:S(2)}) copy-start(bf16[64,256]{1,0:T(8,128)(2,1)} %param.11) | copy-start | bytes 98308
  15.2 38.1 %all-to-all-start = ((bf16[4,32,256]{2,1,0:T(8,128)(2,1)}), bf16[4,32,256]{2,1,0:T(8,128)(2,1)S(1)}, u32[]{:S(2)}, u32[]{:S(2)}) async-start(bf16[4,32,256]{2,1,0:T(8,128)(2,1)} %convert_element_type.70), calls=%async_computation | async-start | bytes 131072 | tf_op jit(solution)/shard_map/all_to_all | solution.py:134
  18.6 31.6 %copy-start.8 = (s32[8]{0:T(128)S(1)}, s32[8]{0:T(128)}, u32[]{:S(2)}) copy-start(s32[8]{0:T(128)} %param.15) | copy-start | bytes 100
  53.3 0.6 copy-start.4
  53.9 38.2 %all-to-all-start.1 = ((bf16[4,32,256]{2,1,0:T(8,128)(2,1)}), bf16[4,32,256]{2,1,0:T(8,128)(2,1)}, u32[]{:S(2)}, u32[]{:S(2)}) async-start(bf16[4,32,256]{2,1,0:T(8,128)(2,1)} %bitcast.29), calls=%async_computation.1 | async-start | bytes 131072 | tf_op jit(solution)/shard_map/all_to_all | solution.py:135
  94.9 2.0 %copy-start = (f32[128,2,4,128]{0,3,2,1:T(8,128)}, f32[128,2,4,128]{0,3,2,1:T(8,128)S(1)}, u32[]{:S(2)}) copy-start(f32[128,2,4,128]{0,3,2,1:T(8,128)S(1)} %get-tuple-element.72) | copy-start | bytes 1572868
  94.9 1.8 %copy-start.5 = (pred[128,128]{0,1:T(8,128)(4,1)S(1)}, pred[128,128]{0,1:T(8,128)(4,1)}, u32[]{:S(2)}) copy-start(pred[128,128]{0,1:T(8,128)(4,1)} %get-tuple-element.67) | copy-start | bytes 49156
  95.7 1.1 %copy-start.6 = (f32[128,2,4]{0,2,1:T(4,128)S(1)}, f32[128,2,4]{0,2,1:T(4,128)}, u32[]{:S(2)}) copy-start(f32[128,2,4]{0,2,1:T(4,128)} %get-tuple-element.75) | copy-start | bytes 12292
  95.7 1.1 %copy-start.3 = (bf16[512,256]{0,1:T(8,128)(2,1)S(1)}, bf16[512,256]{0,1:T(8,128)(2,1)}, u32[]{:S(2)}) copy-start(bf16[512,256]{0,1:T(8,128)(2,1)} %copy.100) | copy-start | bytes 786436
  96.9 2.6 %copy-start.1 = (f32[128,2,4,128]{0,3,2,1:T(8,128)S(1)}, f32[128,2,4,128]{0,3,2,1:T(8,128)}, u32[]{:S(2)}) copy-start(f32[128,2,4,128]{0,3,2,1:T(8,128)} %copy-done) | copy-start | bytes 1572868
where the time goes:
time: 102 us
  blocking collectives  62 us (61%)
  starting transfers between devices  16.1 us (16%)
  local copies, waits for them, and re-layouts  11.1 us (11%)
  matrix products  6.46 us (6%)
  other arithmetic  5.01 us (5%)
    all_gather x1, blocking collectives, body(): values = lax.all_gather(prefix_values, 'seq', axis=0, tiled=True)  31 us
    all_gather x1, blocking collectives, body(): keys = lax.all_gather(prefix_keys, 'seq', axis=0, tiled=True)  31 us
    ppermute x2, starting transfers between devices, from_behind(): return lax.ppermute(array, axis, pairs)  8.92 us
    all_to_all x1, starting transfers between devices, body(): lax.all_to_all(suffix_values, 'tp', split_axis=0, concat_axis=1, tiled=True)  3.89 us
    dot_general x3, matrix products, update(): jnp.einsum('bgrd,kgd->bgrk', q_rot, keys_split, preferred_element_type=jn...  3.34 us
    all_to_all x1, starting transfers between devices, body(): lax.all_to_all(k_rot, 'tp', split_axis=0, concat_axis=1, tiled=True)  3.28 us
    dot_general x3, matrix products, update(): jnp.einsum('bgrk,kgd->bgrd', weights.astype(jnp.bfloat16), values_split,...  3.12 us
    unnamed x23, local copies, waits for them, and re-layouts  2.76 us
  transfers between devices with their start and end apart: 4, of which 0 were waited for; matrix products, arithmetic and copies ran while one was open for 14% of the time, Pallas kernels for 0%

commit v1 on v0

--- a/solution.py
+++ b/solution.py
@@ -107,8 +107,13 @@
         jnp.zeros((rows, kv_heads, repeat, HD), jnp.float32),
     )
     carry = start_state
-    keys = lax.all_gather(prefix_keys, "seq", axis=0, tiled=True)
-    values = lax.all_gather(prefix_values, "seq", axis=0, tiled=True)
+    keys, values = jnp.split(
+        lax.all_gather(
+            jnp.concatenate([prefix_keys, prefix_values], axis=1), "seq", axis=0, tiled=True
+        ),
+        [prefix_keys.shape[1]],
+        axis=1,
+    )
     count = keys.shape[0]
     width = 512
 

time: 102 us -> 69.8 us (0.68)
  blocking collectives: 62 us -> 31.6 us
  matrix products: 6.46 us -> 4.43 us
    all_gather x2 -> x1, blocking collectives: 62 us -> 31.6 us  [body(): lax.all_gather(jnp.concatenate([prefix_keys, prefix_values], axis=1), 'se...]
    dot_general x3, matrix products: 3.12 us -> 1.16 us  [update(): jnp.einsum('bgrk,kgd->bgrd', weights.astype(jnp.bfloat16), values_split,...]
    unnamed x23 -> x30, local copies, waits for them, and re-layouts: 2.76 us -> 2.29 us
  transfers between devices with their start and end apart: 4 -> 4, of which waited for: 0 -> 0; matrix products, arithmetic and copies ran while one was open for 14% -> 19% of each run, Pallas kernels for 0% -> 0%
where the time goes in v1:
time: 69.8 us; the launch traced here: 69.1 us
  blocking collectives  31.6 us (45%)
  starting transfers between devices  16.7 us (24%)
  local copies, waits for them, and re-layouts  10.5 us (15%)
  other arithmetic  4.87 us (7%)
  matrix products  4.43 us (6%)
  between operations  1.02 us (1%)
    all_gather x1, blocking collectives, body(): lax.all_gather(jnp.concatenate([prefix_keys, prefix_values], axis=1), 'se...  31.6 us
    ppermute x2, starting transfers between devices, from_behind(): return lax.ppermute(array, axis, pairs)  8.92 us
    all_to_all x1, starting transfers between devices, body(): lax.all_to_all(suffix_values, 'tp', split_axis=0, concat_axis=1, tiled=True)  3.9 us
    all_to_all x1, starting transfers between devices, body(): lax.all_to_all(k_rot, 'tp', split_axis=0, concat_axis=1, tiled=True)  3.89 us
    dot_general x3, matrix products, update(): jnp.einsum('bgrd,kgd->bgrk', q_rot, keys_split, preferred_element_type=jn...  3.27 us
    unnamed x30, local copies, waits for them, and re-layouts  2.29 us
    convert_element_type x3, local copies, waits for them, and re-layouts, rotate(): return jnp.concatenate([lower * cosine - upper * sine, upper * cosine + l...  1.48 us
    all_to_all x1, local copies, waits for them, and re-layouts, body(): lax.all_to_all(suffix_values, 'tp', split_axis=0, concat_axis=1, tiled=True)  1.47 us
  transfers between devices with their start and end apart: 4, of which 0 were waited for; matrix products, arithmetic and copies ran while one was open for 19% of the time, Pallas kernels for 0%

profile of v1, /device:TPU:0, one launch (start us, length us, event | category | flops | bytes accessed | tf_op | source)
XLA Modules:
  0.0 69.1 jit_solution(6173528633228958570)
XLA Ops:
  0.7 0.8 %copy.100 = s32[24,1]{1,0:T(8,128)S(1)} copy(s32[24,1]{0,1:T(1,128)} %bitcast.108) | data formatting | bytes 192 | tf_op jit(solution)/shard_map/reshape.328
  1.5 0.1 reduce
  1.6 0.7 sub.87
  2.4 0.7 %select_reduce_fusion.2 = (s32[128]{0:T(128)S(1)}, s32[128]{0:T(128)S(1)}) fusion(s32[24]{0:T(128)} %param.14, s32[128]{0:T(128)S(1)} %get-tuple-element.49, s32[24]{0:T(128)S(1)} %sub.87), kind=kLoop, calls=%fused_computation.55 | loop fusion | flops 15104 | bytes 1728 | tf_op jit(solution)/shard_map/reduce_sum | solution.py:39
  3.1 0.9 %copy.107 = bf16[128,256]{0,1:T(8,128)(2,1)S(1)} copy(bf16[128,256]{1,0:T(8,128)(2,1)} %param.9) | data formatting | bytes 131072 | tf_op args[1]
  4.3 0.3 multiply_cosine_fusion
  4.7 0.7 %copy.112 = bf16[128,2,128]{0,2,1:T(8,128)(2,1)} copy(bf16[128,2,128]{2,0,1:T(8,128)(2,1)S(1)} %maximum_convert_fusion) | data formatting | bytes 131072 | tf_op jit(solution)/shard_map/convert_element_type | solution.py:31
  5.5 5.5 %collective-permute-start = (bf16[128,256]{0,1:T(8,128)(2,1)}, bf16[128,256]{0,1:T(8,128)(2,1)}, u32[]{:S(2)}, u32[]{:S(2)}) collective-permute-start(bf16[128,256]{0,1:T(8,128)(2,1)} %bitcast.19), channel_id=1, source_target_pairs={{0,4},{4,8},{8,12},{12,16},{16,20},{20,24},{24,28},{1,5},{5,9},{9,... | collective-permute-start | bytes 196616 | tf_op jit(solution)/shard_map/ppermute | solution.py:15
  10.9 3.5 %collective-permute-start.1 = (bf16[128,256]{1,0:T(8,128)(2,1)}, bf16[128,256]{1,0:T(8,128)(2,1)}, u32[]{:S(2)}, u32[]{:S(2)}) collective-permute-start(bf16[128,256]{1,0:T(8,128)(2,1)} %param.10), channel_id=1, source_target_pairs={{0,4},{4,8},{8,12},{12,16},{16,20},{20,24},{24,28},{1,5},{5,9},{9,... | collective-permute-start | bytes 196616 | tf_op jit(solution)/shard_map/ppermute | solution.py:15
  14.5 0.7 convert_element_type.70
  15.2 3.9 %all-to-all-start = ((bf16[4,32,256]{2,1,0:T(8,128)(2,1)}), bf16[4,32,256]{2,1,0:T(8,128)(2,1)}, u32[]{:S(2)}, u32[]{:S(2)}) async-start(bf16[4,32,256]{2,1,0:T(8,128)(2,1)} %convert_element_type.70), calls=%async_computation | async-start | bytes 131072 | tf_op jit(solution)/shard_map/all_to_all | solution.py:139
  19.3 0.2 fusion.45
  19.5 31.6 %all_gather.3 = bf16[512,512]{1,0:T(8,128)(2,1)S(1)} all-gather(bf16[64,512]{1,0:T(8,128)(2,1)S(1)} %pad_maximum_fusion.1), channel_id=1, replica_groups=mesh['seq'=8,'tp'=4] {'seq'}, dimensions={0}, use_global_device_ids=true | all-gather | bytes 589824 | tf_op jit(solution)/shard_map/all_gather | solution.py:111
  51.2 0.1 copy.134
  51.3 0.2 subtract_convert_fusion
  51.6 0.1 broadcast_compare_fusion
  51.8 1.2 %fusion = (f32[128,2,4]{0,2,1:T(4,128)}, f32[2,512,128,4]{2,1,3,0:T(8,128)S(1)}) fusion(pred[128,512]{0,1:T(8,128)(4,1)S(1)} %broadcast_compare_fusion, bf16[512,2,128,1]{0,2,3,1:T(8,128)(2,1)S(1)} %bitcast.100, bf16[128,2,4,64]{3,0,2,1:T(8,128)(2,1)S(1)} %bitcast.97, bf16[128,2,4,64]{3,0,2,1:T(8,128)(2,1)S(1)} %bitcast.94), kind=kOutput, calls=%fused_computation.2 | convolution fusion | flops 136313856 | bytes 2691072 | tf_op jit(solution)/shard_map/while/body/eval_jaxpr/bgrd,kgd->bgrk/dot_general | solution.py:75
  52.9 0.8 %compare_and_fusion = (pred[128,128]{0,1:T(8,128)(4,1)}, pred[128,128]{0,1:T(8,128)(4,1)S(1)}) fusion(s32[128]{0:T(128)S(1)} %get-tuple-element.80, s32[128]{0:T(128)S(1)} %get-tuple-element.49, s32[128]{0:T(128)S(1)} %get-tuple-element.79, s32[128]{0:T(128)S(1)} %get-tuple-element.48, pred[128]{0:T(512)(128)(4,1)S(1)} %get-tuple-element.81, ...), kind=kLoop, calls=%fused_computation.49 | loop fusion | flops 131072 | bytes 35072 | tf_op jit(solution)/shard_map/and | solution.py:99
  53.7 3.9 %all-to-all-start.1 = ((bf16[4,32,256]{2,1,0:T(8,128)(2,1)}), bf16[4,32,256]{2,1,0:T(8,128)(2,1)}, u32[]{:S(2)}, u32[]{:S(2)}) async-start(bf16[4,32,256]{2,1,0:T(8,128)(2,1)} %bitcast.29), calls=%async_computation.1 | async-start | bytes 131072 | tf_op jit(solution)/shard_map/all_to_all | solution.py:140
  57.6 0.9 %fusion.48 = (f32[128,2,4]{0,2,1:T(4,128)}, f32[128,2,4,128]{0,3,2,1:T(8,128)S(1)}) fusion(bf16[128,2,4,64]{3,0,2,1:T(8,128)(2,1)S(1)} %bitcast.98, bf16[128,2,4,64]{3,0,2,1:T(8,128)(2,1)S(1)} %bitcast.95, bf16[128,2,128]{2,0,1:T(8,128)(2,1)S(1)} %maximum_convert_fusion, pred[128,128]{0,1:T(8,128)(4,1)S(1)} %get-tuple-element.70), kind=kOutput, calls=%fused_computation.88 | convolution fusion | flops 34470912 | bytes 872448 | tf_op jit(solution)/shard_map/bgrd,kgd->bgrk/dot_general | solution.py:75
  58.5 0.9 %copy.131 = bf16[128,256]{0,1:T(8,128)(2,1)S(1)} copy(bf16[128,256]{1,0:T(8,128)(2,1)} %param.10) | data formatting | bytes 131072 | tf_op jit(solution)/shard_map/reshape | solution.py:73
  59.4 0.8 %copy.105 = bf16[512,256]{0,1:T(8,128)(2,1)} copy(bf16[512,256]{1,0:T(8,128)(2,1)S(1)} %get-tuple-element.59) | data formatting | bytes 524288 | tf_op jit(solution)/shard_map/split | solution.py:110
  60.3 1.5 %copy.139 = bf16[4,4,8,256]{3,2,0,1:T(8,128)(2,1)} copy(bf16[4,4,8,256]{3,2,1,0:T(8,128)(2,1)} %bitcast.44) | data formatting | bytes 131072 | tf_op jit(solution)/shard_map/all_to_all | solution.py:139
  61.8 1.5 %copy.140 = bf16[4,4,8,256]{3,2,0,1:T(8,128)(2,1)} copy(bf16[4,4,8,256]{3,2,1,0:T(8,128)(2,1)} %bitcast.46) | data formatting | bytes 131072 | tf_op jit(solution)/shard_map/all_to_all | solution.py:140
  63.2 1.2 %fusion.47 = (f32[128,2,4]{0,2,1:T(4,128)S(1)}, f32[128,2,4,128]{0,3,2,1:T(8,128)S(1)}) fusion(bf16[128,2,128,1]{0,2,3,1:T(8,128)(2,1)} %bitcast.39, bf16[128,2,4,64]{3,0,2,1:T(8,128)(2,1)S(1)} %bitcast.99, bf16[128,2,4,64]{3,0,2,1:T(8,128)(2,1)S(1)} %bitcast.96, pred[128,128]{0,1:T(8,128)(4,1)} %get-tuple-element.69), kind=kOutput, calls=%fused_computation.87 | convolution fusion | flops 34470912 | bytes 872448 | tf_op jit(solution)/shard_map/bgrd,kgd->bgrk/dot_general | solution.py:75
  64.5 0.7 %fusion.42 = (f32[128,2,4]{0,2,1:T(4,128)S(1)}, f32[128,2,4]{0,2,1:T(4,128)S(1)}, f32[128,2,4]{0,2,1:T(4,128)S(1)}, f32[128,2,4]{0,2,1:T(4,128)S(1)}) fusion(f32[128,2,4]{0,2,1:T(4,128)S(1)} %get-tuple-element.73, f32[128,2,4]{0,2,1:T(4,128)} %get-tuple-element.75, f32[128,2,4]{0,2,1:T(4,128)} %get-tuple-element.77), kind=kLoop, calls=%fused_computation.83 | loop fusion | flops 5120 | bytes 28672 | tf_op jit(solution)/shard_map/max | solution.py:80
  65.4 0.2 convolution_bitcast_fusion.1
  65.6 0.5 fusion.1
  66.3 0.7 fusion.6
  67.0 0.9 %copy.114 = bf16[128,256]{0,1:T(8,128)(2,1)S(1)} copy(bf16[128,256]{1,0:T(8,128)(2,1)} %collective-permute-done.1) | data formatting | bytes 131072 | tf_op jit(solution)/shard_map/ppermute | solution.py:15
  68.0 0.3 fusion.13
  68.3 0.9 %copy.119 = bf16[128,1024]{1,0:T(8,128)(2,1)} copy(bf16[128,1024]{0,1:T(8,128)(2,1)S(1)} %bitcast.104) | data formatting | bytes 524288
  (49 shorter events, 1.2 us)
Async XLA Ops:
  0.6 18.5 %copy-start.2 = (bf16[128,1024]{1,0:T(8,128)(2,1)S(1)}, bf16[128,1024]{1,0:T(8,128)(2,1)}, u32[]{:S(2)}) copy-start(bf16[128,1024]{1,0:T(8,128)(2,1)} %param.8) | copy-start | bytes 786436
  5.5 57.8 %collective-permute-start = (bf16[128,256]{0,1:T(8,128)(2,1)}, bf16[128,256]{0,1:T(8,128)(2,1)}, u32[]{:S(2)}, u32[]{:S(2)}) collective-permute-start(bf16[128,256]{0,1:T(8,128)(2,1)} %bitcast.19), channel_id=1, source_target_pairs={{0,4},{4,8},{8,12},{12,16},{16,20},{20,24},{24,28},{1,5},{5,9},{9,... | collective-permute-start | bytes 196616 | tf_op jit(solution)/shard_map/ppermute | solution.py:15
  10.9 56.1 %collective-permute-start.1 = (bf16[128,256]{1,0:T(8,128)(2,1)}, bf16[128,256]{1,0:T(8,128)(2,1)}, u32[]{:S(2)}, u32[]{:S(2)}) collective-permute-start(bf16[128,256]{1,0:T(8,128)(2,1)} %param.10), channel_id=1, source_target_pairs={{0,4},{4,8},{8,12},{12,16},{16,20},{20,24},{24,28},{1,5},{5,9},{9,... | collective-permute-start | bytes 196616 | tf_op jit(solution)/shard_map/ppermute | solution.py:15
  14.5 5.0 %copy-start.9 = (bf16[64,256]{1,0:T(8,128)(2,1)S(1)}, bf16[64,256]{1,0:T(8,128)(2,1)}, u32[]{:S(2)}) copy-start(bf16[64,256]{1,0:T(8,128)(2,1)} %param.12) | copy-start | bytes 98308
  14.5 5.0 %copy-start.10 = (bf16[64,256]{1,0:T(8,128)(2,1)S(1)}, bf16[64,256]{1,0:T(8,128)(2,1)}, u32[]{:S(2)}) copy-start(bf16[64,256]{1,0:T(8,128)(2,1)} %param.11) | copy-start | bytes 98308
  15.2 38.5 %all-to-all-start = ((bf16[4,32,256]{2,1,0:T(8,128)(2,1)}), bf16[4,32,256]{2,1,0:T(8,128)(2,1)}, u32[]{:S(2)}, u32[]{:S(2)}) async-start(bf16[4,32,256]{2,1,0:T(8,128)(2,1)} %convert_element_type.70), calls=%async_computation | async-start | bytes 131072 | tf_op jit(solution)/shard_map/all_to_all | solution.py:139
  19.5 32.0 %copy-start.11 = (s32[8]{0:T(128)S(1)}, s32[8]{0:T(128)}, u32[]{:S(2)}) copy-start(s32[8]{0:T(128)} %param.15) | copy-start | bytes 100
  53.7 8.1 %all-to-all-start.1 = ((bf16[4,32,256]{2,1,0:T(8,128)(2,1)}), bf16[4,32,256]{2,1,0:T(8,128)(2,1)}, u32[]{:S(2)}, u32[]{:S(2)}) async-start(bf16[4,32,256]{2,1,0:T(8,128)(2,1)} %bitcast.29), calls=%async_computation.1 | async-start | bytes 131072 | tf_op jit(solution)/shard_map/all_to_all | solution.py:140
  64.5 1.8 %copy-start = (f32[128,2,4,128]{0,3,2,1:T(8,128)}, f32[128,2,4,128]{0,3,2,1:T(8,128)S(1)}, u32[]{:S(2)}) copy-start(f32[128,2,4,128]{0,3,2,1:T(8,128)S(1)} %get-tuple-element.74) | copy-start | bytes 1572868
  64.5 1.7 %copy-start.4 = (pred[128,128]{0,1:T(8,128)(4,1)S(1)}, pred[128,128]{0,1:T(8,128)(4,1)}, u32[]{:S(2)}) copy-start(pred[128,128]{0,1:T(8,128)(4,1)} %get-tuple-element.69) | copy-start | bytes 49156
  65.2 1.1 %copy-start.7 = (f32[128,2,4]{0,2,1:T(4,128)}, f32[128,2,4]{0,2,1:T(4,128)S(1)}, u32[]{:S(2)}) copy-start(f32[128,2,4]{0,2,1:T(4,128)S(1)} %get-tuple-element.55) | copy-start | bytes 12292
  65.2 1.1 %copy-start.6 = (f32[128,2,4]{0,2,1:T(4,128)S(1)}, f32[128,2,4]{0,2,1:T(4,128)}, u32[]{:S(2)}) copy-start(f32[128,2,4]{0,2,1:T(4,128)} %get-tuple-element.77) | copy-start | bytes 12292
  65.2 1.1 %copy-start.3 = (bf16[512,256]{0,1:T(8,128)(2,1)S(1)}, bf16[512,256]{0,1:T(8,128)(2,1)}, u32[]{:S(2)}) copy-start(bf16[512,256]{0,1:T(8,128)(2,1)} %copy.105) | copy-start | bytes 786436
  66.3 1.7 %copy-start.1 = (f32[128,2,4,128]{0,3,2,1:T(8,128)S(1)}, f32[128,2,4,128]{0,3,2,1:T(8,128)}, u32[]{:S(2)}) copy-start(f32[128,2,4,128]{0,3,2,1:T(8,128)} %copy-done) | copy-start | bytes 1572868
  66.3 1.7 %copy-start.5 = (pred[128,128]{0,1:T(8,128)(4,1)S(1)}, pred[128,128]{0,1:T(8,128)(4,1)}, u32[]{:S(2)}) copy-start(pred[128,128]{0,1:T(8,128)(4,1)} %get-tuple-element.69) | copy-start | bytes 49156
  66.3 1.7 %copy-start.8 = (f32[128,2,4]{0,2,1:T(4,128)S(1)}, f32[128,2,4]{0,2,1:T(4,128)}, u32[]{:S(2)}) copy-start(f32[128,2,4]{0,2,1:T(4,128)} %copy-done.7) | copy-start | bytes 12292
